TPU v7x, 32 devices: a whole 2x2x4 slice. The times are simulated.
32 devices in a mesh: groups: 2 (over x), heads: 4 (over y, core), seq: 4 (over z).
Axes of the slice: x: 2, y: 2, z: 4, core: 2. Of those that a mesh axis runs over, the one named last changes fastest.
Arguments:
- lin_query: bfloat16 [4096, 4096], P(('groups', 'seq'), 'heads'), parts along dimension 0, may hold values from -6 to 6
- lin_key: bfloat16 [4096, 4096], P(('groups', 'seq'), 'heads'), parts along dimension 0, may hold values from -6 to 6
- lin_value: bfloat16 [4096, 4096], P(('groups', 'seq'), 'heads'), parts along dimension 0, may hold values from -6 to 6
- log_decay: float32 [4096, 32], P(('groups', 'seq'), 'heads'), parts along dimension 0, may hold values from -1 to 0
- stream: bfloat16 [4096, 6144], P(('groups', 'seq'), 'heads'), parts along dimension 0, may hold values from -400 to 400
- out_weight: bfloat16 [4096, 6144], P('heads', 'seq'), may hold values from -0.125 to 0.125
- norm_gain: bfloat16 [6144], P('heads'), may hold values from 0.5 to 1.5
- query_weight: bfloat16 [6144, 4096], P('seq', 'heads'), may hold values from -12 to 12
- kv_weight: bfloat16 [4, 6144, 256], P(None, 'seq'), may hold values from -1 to 1
Outputs:
- stream_next: bfloat16 [4096, 6144], P(('groups', 'seq'), 'heads'), parts along dimension 0
- attended: bfloat16 [4096, 4096], P(('groups', 'seq'), 'heads'), parts along dimension 0
There are 2 independent parts, one for each index of `groups`. A program takes and returns all parts, laid end to end along the dimension named above; an argument that names none is the same for every part. Nothing has to cross between parts.
All inputs are finite; a program needn't handle non-finite values.
Results may differ from a plain program's by a relative error of at most 0.019.
Values may be sent and summed in bfloat16 or wider, within the bound.
No kernel may reach another device: no remote copies, remote signals or barrier semaphores. Data moves between devices by JAX's collectives and lax.ppermute only.
A program may use at most 128 MiB of HBM per device.

v0:
```python
import jax
import jax.numpy as jnp
from jax import lax
from jax.sharding import PartitionSpec as P

D = 6144
QUERY_HEADS = 32
KVH = 4
DH = 128
BLOCK = 256


def from_behind(value, axis, steps):
    count = lax.axis_size(axis)
    leading, last = (max(0, -steps), min(count, count - steps))
    return lax.ppermute(value, axis, [(source, source + steps) for source in range(leading, last)])


def lightning_block(kv_state, block_inputs):
    query_blk, key_blk, value_blk, decay_blk = block_inputs
    block_len = query_blk.shape[0]
    local_cum = jnp.cumsum(decay_blk, axis=0)
    causal_mask = (jnp.arange(block_len)[:, None] >= jnp.arange(block_len)[None, :])[:, :, None]
    decay_diff = local_cum[:, None, :] - local_cum[None, :, :]
    decays = jnp.where(causal_mask, jnp.exp(jnp.where(causal_mask, decay_diff, 0.0)), 0.0)
    scores = jnp.einsum("thd,shd->hts", query_blk, key_blk, preferred_element_type=jnp.float32)
    weights = (scores * jnp.transpose(decays, (2, 0, 1))).astype(jnp.bfloat16)
    intra_out = jnp.einsum("hts,shd->thd", weights, value_blk, preferred_element_type=jnp.float32)
    query_f = query_blk.astype(jnp.float32)
    inter_out = jnp.einsum(
        "thd,hde->the",
        query_f * jnp.exp(local_cum)[:, :, None],
        kv_state,
        precision=lax.Precision.HIGHEST,
    )
    tail_decay = jnp.exp(local_cum[-1][None, :] - local_cum)
    key_f = key_blk.astype(jnp.float32) * tail_decay[:, :, None]
    kv_state = jnp.exp(local_cum[-1])[:, None, None] * kv_state + jnp.einsum(
        "shd,she->hde", key_f, value_blk.astype(jnp.float32), precision=lax.Precision.HIGHEST
    )
    return (kv_state, intra_out + inter_out)


def shards(
    lin_query, lin_key, lin_value, log_decay, stream, out_weight, norm_gain, query_weight, kv_weight
):
    tok_rows = lin_query.shape[0]
    heads_here = log_decay.shape[1]
    head_width = heads_here * DH
    nblocks = tok_rows // BLOCK
    block_shape = (nblocks, BLOCK, heads_here, DH)
    inputs = (
        lin_query.reshape(block_shape),
        lin_key.reshape(block_shape),
        lin_value.reshape(block_shape),
        log_decay.reshape(nblocks, BLOCK, heads_here),
    )
    start_state = jnp.zeros((heads_here, DH, DH), jnp.float32)
    local_state, local_out = lax.scan(lightning_block, start_state, inputs)
    local_out = local_out.reshape(tok_rows, heads_here, DH)
    decay_total = jnp.sum(log_decay, axis=0)
    totals, states = (
        lax.all_gather(decay_total[None].astype(jnp.bfloat16), "seq", axis=0, tiled=True).astype(
            jnp.float32
        ),
        lax.all_gather(local_state[None].astype(jnp.bfloat16), "seq", axis=0, tiled=True).astype(
            jnp.float32
        ),
    )
    position = lax.axis_index("seq")
    device_order = jnp.arange(totals.shape[0])
    earlier = (device_order < position)[:, None]
    before = jnp.sum(jnp.where(earlier, totals, 0.0), axis=0)
    inclusive = jnp.cumsum(totals, axis=0)
    factors = jnp.where(earlier, jnp.exp(jnp.where(earlier, before[None, :] - inclusive, 0.0)), 0.0)
    incoming = jnp.einsum("jh,jhde->hde", factors, states, precision=lax.Precision.HIGHEST)
    running = jnp.cumsum(log_decay, axis=0)
    query_f = (
        lin_query.reshape(tok_rows, heads_here, DH).astype(jnp.float32)
        * jnp.exp(running)[:, :, None]
    )
    carried = jnp.einsum("thd,hde->the", query_f, incoming, precision=lax.Precision.HIGHEST)
    lin_raw = local_out + carried
    lin_out = (
        (lin_raw * lax.rsqrt(jnp.mean(lin_raw * lin_raw, axis=-1, keepdims=True) + 1e-06))
        .astype(jnp.bfloat16)
        .reshape(tok_rows, head_width)
    )
    branch = jnp.dot(
        lin_out,
        lax.all_gather(out_weight, "seq", axis=1, tiled=True),
        preferred_element_type=jnp.float32,
    )
    kv_group = lax.axis_index("heads") * heads_here // (QUERY_HEADS // KVH)
    kv_mine = lax.dynamic_index_in_dim(kv_weight, kv_group, 0, keepdims=False)
    query_rows, kv_rows = (
        lax.all_gather(query_weight, "seq", axis=0, tiled=True),
        lax.all_gather(kv_mine, "seq", axis=0, tiled=True),
    )
    projection = jnp.concatenate([query_rows, kv_rows], axis=1)
    own_sum = lax.psum_scatter(
        branch.astype(jnp.bfloat16), "heads", scatter_dimension=1, tiled=True
    ).astype(jnp.float32)
    mixed_sum = stream.astype(jnp.float32) + own_sum
    stream_next = mixed_sum.astype(jnp.bfloat16)
    total_sq = lax.psum(jnp.sum(mixed_sum * mixed_sum, axis=1), "heads")
    normed = (
        mixed_sum
        * lax.rsqrt(total_sq / D + 1e-05)[:, None]
        * norm_gain.astype(jnp.float32)[None, :]
    ).astype(jnp.bfloat16)
    projected = jnp.dot(
        lax.all_gather(normed, "heads", axis=1, tiled=True),
        projection,
        preferred_element_type=jnp.float32,
    )
    projected = projected.astype(jnp.bfloat16)
    queries = projected[:, :head_width].reshape(tok_rows, heads_here, DH)
    keys_values = projected[:, head_width:]
    position = lax.axis_index("seq")
    query_pos = position * tok_rows + jnp.arange(tok_rows)
    score_scale = float(DH) ** (-0.5)

    def attend(state_in, kv_block, key_start):
        old_max, row_total, weighted = state_in
        key_count = kv_block.shape[0]
        key_part = kv_block[:, :DH]
        value_part = kv_block[:, DH:]
        scores = (
            jnp.einsum("thd,sd->hts", queries, key_part, preferred_element_type=jnp.float32)
            * score_scale
        )
        key_pos = key_start + jnp.arange(key_count)
        allowed = ((key_pos[None, :] <= query_pos[:, None]) & (key_pos[None, :] >= 0))[None, :, :]
        scores = jnp.where(allowed, scores, -1e30)
        new_max = jnp.maximum(old_max, jnp.max(scores, axis=-1))
        expos = jnp.where(allowed, jnp.exp(scores - new_max[:, :, None]), 0.0)
        rescale = jnp.exp(old_max - new_max)
        row_total = row_total * rescale + jnp.sum(expos, axis=-1)
        prob_bf16 = expos.astype(jnp.bfloat16)
        weighted = weighted * rescale[:, :, None] + jnp.einsum(
            "hts,sd->htd", prob_bf16, value_part, preferred_element_type=jnp.float32
        )
        return (new_max, row_total, weighted)

    initial = (
        jnp.full((heads_here, tok_rows), -1e30, jnp.float32),
        jnp.zeros((heads_here, tok_rows), jnp.float32),
        jnp.zeros((heads_here, tok_rows, DH), jnp.float32),
    )
    first_state = attend(initial, keys_values, position * tok_rows)
    seq_count = lax.axis_size("seq")

    def cycle_turn(turn_index, loop_state):
        moving, inner_state = loop_state
        moving = from_behind(moving, "seq", 1)
        source = position - turn_index
        return (moving, attend(inner_state, moving, source * tok_rows))

    _, final_state = lax.fori_loop(1, seq_count, cycle_turn, (keys_values, first_state))
    _, row_total, weighted = final_state
    attended = (
        jnp.transpose(weighted / row_total[:, :, None], (1, 0, 2))
        .reshape(tok_rows, head_width)
        .astype(jnp.bfloat16)
    )
    return (stream_next, attended)


def solution(mesh):
    return jax.shard_map(
        shards,
        mesh=mesh,
        in_specs=(
            P(("groups", "seq"), "heads"),
            P(("groups", "seq"), "heads"),
            P(("groups", "seq"), "heads"),
            P(("groups", "seq"), "heads"),
            P(("groups", "seq"), "heads"),
            P("heads", "seq"),
            P("heads"),
            P("seq", "heads"),
            P(None, "seq", None),
        ),
        out_specs=(P(("groups", "seq"), "heads"), P(("groups", "seq"), "heads")),
        check_vma=False,
    )
```

profile of v0, /device:TPU:0, one launch (start us, length us, event | category | flops | bytes accessed | tf_op | source)
XLA Modules:
  0.0 828.3 jit_solution(3079648835785859866)
XLA Ops:
  7.3 2.6 copy.92
  9.9 2.5 copy.93
  13.6 79.9 %while.34 = (s32[]{:T(128)}, f32[8,128,128]{2,1,0:T(8,128)}, f32[2,256,8,128]{1,0,3,2:T(2,128)}, f32[2,256,8]{1,2,0:T(8,128)S(1)}, bf16[2,256,8,128]{3,2,1,0:T(8...) while((s32[]{:T(128)}, f32[8,128,128]{2,1,0:T(8,128)}, ...), condition=%wide.region_3.4_spmd.clone, body=%wide.region_0.3_spmd.clone.sunk | while | flops 1078530048 | bytes 19645352 | solution.py:59
  14.5 2.3 constant_dynamic-slice_fusion.7
  16.8 3.5 convolution_bitcast_fusion.2
  21.6 2.2 convolution_add_fusion.2
  23.9 3.8 fusion.84
  27.7 3.3 copy.136
  31.0 22.0 %dynamic_update_slice.6 = f32[2,256,8,128]{1,0,3,2:T(2,128)} dynamic-update-slice(f32[2,256,8,128]{1,0,3,2:T(2,128)} %get-tuple-element.452, f32[1,256,8,128]{1,0,3,2:T(1,128)} %copy.136, s32[]{:T(128)S(6)} %copy.141, s32[]{:T(128)} %constant.109.clone.1..sunk, s32[]{:T(128)} %constant.109.clone.1..sunk, s32[]{:T(128)} %constant.109.clone.1..sunk) | dynamic-update-slice | bytes 2097156 | tf_op jit(solution)/shard_map/while/body/jit(dynamic_update_index_in_dim)/dynamic_update_slice | solution.py:59
  53.8 2.3 constant_dynamic-slice_fusion.7
  56.0 3.7 convolution_bitcast_fusion.2
  61.1 3.4 convolution_add_fusion.2
  64.5 3.8 fusion.84
  68.3 3.3 copy.136
  71.6 22.0 %dynamic_update_slice.6 = f32[2,256,8,128]{1,0,3,2:T(2,128)} dynamic-update-slice(f32[2,256,8,128]{1,0,3,2:T(2,128)} %get-tuple-element.452, f32[1,256,8,128]{1,0,3,2:T(1,128)} %copy.136, s32[]{:T(128)S(6)} %copy.141, s32[]{:T(128)} %constant.109.clone.1..sunk, s32[]{:T(128)} %constant.109.clone.1..sunk, s32[]{:T(128)} %constant.109.clone.1..sunk) | dynamic-update-slice | bytes 2097156 | tf_op jit(solution)/shard_map/while/body/jit(dynamic_update_index_in_dim)/dynamic_update_slice | solution.py:59
  93.5 1.8 convert_element_type.87
  96.3 3.9 reshape.219
  101.7 14.2 %all-reduce = bf16[32]{0:T(256)(128)(2,1)S(1)} all-reduce(bf16[32]{0:T(256)(128)(2,1)S(1)} %dynamic-update-slice), channel_id=2, replica_groups=mesh['groups'=2,'heads'=4,'seq'=4] {'seq'}, use_global_device_ids=true, to_apply=%add | all-reduce | flops 32 | bytes 128
  117.6 8.8 %all-gather.15.cloned.1.call-done = bf16[32,128,128]{2,1,0:T(8,128)(2,1)} async-done(((bf16[8,128,128]{2,1,0:T(8,128)(2,1)}), bf16[32,128,128]{2,1,0:T(8,128)(2,1)}) %all-gather.15.cloned.1.call-update) | async-done | bytes 1048592 | tf_op jit(solution)/shard_map/all_gather | solution.py:66
  126.4 1.6 multiply_reduce_fusion.1
  127.9 4.7 multiply_reduce_fusion.2
  133.9 211.7 %all-gather.9.cloned.1.call-done = bf16[1024,6144]{1,0:T(8,128)(2,1)} async-done(((bf16[1024,1536]{1,0:T(8,128)(2,1)}), bf16[1024,6144]{1,0:T(8,128)(2,1)}) %all-gather.9.cloned.1.call-update) | async-done | bytes 12582928 | tf_op jit(solution)/shard_map/all_gather | solution.py:91
  345.6 11.8 %convolution_convert_fusion = bf16[512,6144]{1,0:T(8,128)(2,1)} fusion(bf16[512,1024]{0,1:T(8,128)(2,1)} %bitcast.181, bf16[1024,6144]{1,0:T(8,128)(2,1)} %all-gather.9.cloned.1.call-done), kind=kOutput, calls=%fused_computation.60 | convolution fusion | flops 6445596672 | bytes 19922944 | tf_op jit(solution)/shard_map/dot_general | solution.py:89
  359.1 54.5 %reduce-scatter.2.cloned.1.call-done = bf16[512,1536]{1,0:T(8,128)(2,1)} async-done(((bf16[512,6144]{1,0:T(8,128)(2,1)}), bf16[512,1536]{1,0:T(8,128)(2,1)}) %reduce-scatter.2.cloned.1.call-update) | async-done | bytes 1572880 | tf_op jit(solution)/shard_map/reduce_scatter | solution.py:101
  413.7 2.1 multiply_reduce_fusion
  415.8 6.0 psum.7
  421.8 2.3 multiply_convert_fusion.1
  424.4 54.7 %all-gather.17.cloned.1.call-done = bf16[1,6144,256]{2,1,0:T(8,128)(2,1)} async-done(((bf16[1,1536,256]{2,1,0:T(8,128)(2,1)}), bf16[1,6144,256]{2,1,0:T(8,128)(2,1)}) %all-gather.17.cloned.1.call-update) | async-done | bytes 3145744 | tf_op jit(solution)/shard_map/all_gather | solution.py:98
  479.1 218.3 %all-gather.13.cloned.1.call-done = bf16[6144,1024]{1,0:T(8,128)(2,1)} async-done(((bf16[1536,1024]{1,0:T(8,128)(2,1)}), bf16[6144,1024]{1,0:T(8,128)(2,1)}) %all-gather.13.cloned.1.call-update) | async-done | bytes 12582928 | tf_op jit(solution)/shard_map/all_gather | solution.py:97
  697.4 46.0 %all-gather.11.cloned.1.call-done = bf16[512,6144]{1,0:T(8,128)(2,1)} async-done(((bf16[512,1536]{1,0:T(8,128)(2,1)}), bf16[512,6144]{1,0:T(8,128)(2,1)}) %all-gather.11.cloned.1.call-update) | async-done | bytes 6291472 | tf_op jit(solution)/shard_map/all_gather | solution.py:113
  743.4 15.6 %fusion.43 = bf16[512,1280]{1,0:T(8,128)(2,1)S(1)} fusion(bf16[512,6144]{1,0:T(8,128)(2,1)} %all-gather.11.cloned.1.call-done, bf16[6144,256]{1,0:T(8,128)(2,1)} %bitcast.188, bf16[6144,1024]{1,0:T(8,128)(2,1)} %all-gather.13.cloned.1.call-done), kind=kOutput, calls=%fused_computation.71 | convolution fusion | flops 8085176320 | bytes 23330816 | tf_op jit(solution)/shard_map/dot_general | solution.py:112
  759.2 1.5 fusion.37
  760.7 2.0 fusion.39
  762.8 3.9 fusion.49
  766.7 51.9 %while.33 = (s32[]{:T(128)}, bf16[512,256]{1,0:T(8,128)(2,1)S(1)}, f32[8,512]{1,0:T(8,128)S(1)}, f32[8,512]{1,0:T(8,128)S(1)}, f32[8,512,128]{2,1,0:T(8,128)}, /...) while((s32[]{:T(128)}, bf16[512,256]{1,0:T(8,128)(2,1)S(1)}, ...), condition=%wide.region_18.19_spmd.clone, body=%wide.region_15.18_spmd.clone.sunk | while | flops 1102587904 | bytes 50341096 | solution.py:160
  766.7 3.4 collective-permute-start
  770.4 5.7 collective-permute-done
  777.6 2.0 fusion.79
  779.7 3.1 multiply_add_fusion.5
  784.2 4.4 collective-permute-start
  788.9 4.8 collective-permute-done
  795.3 2.0 fusion.79
  797.4 3.1 multiply_add_fusion.5
  801.8 4.4 collective-permute-start
  806.5 3.9 collective-permute-done
  812.0 2.0 fusion.79
  814.1 3.1 multiply_add_fusion.5
  818.6 2.9 copy_bitcast_fusion.11
  (125 shorter events, 22.3 us)
Async XLA Ops:
  7.2 350.3 %copy-start = (bf16[4,1536,256]{2,1,0:T(8,128)(2,1)S(1)}, bf16[4,1536,256]{2,1,0:T(8,128)(2,1)}, u32[]{:S(2)}) copy-start(bf16[4,1536,256]{2,1,0:T(8,128)(2,1)} %param.21) | copy-start | bytes 9437188
  7.2 119.2 %all-gather.15.cloned.1.call-start = ((), (), s32[]{:S(2)}) async-start(), calls=%async_computation.5 | async-start | bytes 1310720 | tf_op jit(solution)/shard_map/all_gather | solution.py:66
  7.2 5.1 copy-start.6
  7.3 6.4 copy-start.9
  16.7 4.9 copy-start.2
  21.6 2.2 copy-start.3
  56.0 5.0 copy-start.2
  61.0 3.4 copy-start.3
  95.3 4.9 copy-start.11
  95.4 250.2 %all-gather.9.cloned.1.call-start = ((), (), s32[]{:S(2)}) async-start(), calls=%async_computation.1 | async-start | bytes 15728640 | tf_op jit(solution)/shard_map/all_gather | solution.py:91
  96.1 317.6 %reduce-scatter.2.cloned.1.call-start = ((), (), s32[]{:S(2)}) async-start(), calls=%async_computation.2 | async-start | bytes 7864320 | tf_op jit(solution)/shard_map/reduce_scatter | solution.py:101
  357.4 1.7 copy-start.10
  357.4 121.7 %all-gather.17.cloned.1.call-start = ((), (), s32[]{:S(2)}) async-start(), calls=%async_computation.6 | async-start | bytes 3932160 | tf_op jit(solution)/shard_map/all_gather | solution.py:98
  358.4 55.2 %copy-start.4 = (bf16[512,1536]{1,0:T(8,128)(2,1)S(1)}, bf16[512,1536]{1,0:T(8,128)(2,1)}, u32[]{:S(2)}) copy-start(bf16[512,1536]{1,0:T(8,128)(2,1)} %param.17) | copy-start | bytes 4718596
  358.5 338.9 %all-gather.13.cloned.1.call-start = ((), (), s32[]{:S(2)}) async-start(), calls=%async_computation.4 | async-start | bytes 15728640 | tf_op jit(solution)/shard_map/all_gather | solution.py:97
  359.1 384.3 %all-gather.11.cloned.1.call-start = ((), (), s32[]{:S(2)}) async-start(), calls=%async_computation.3 | async-start | bytes 7864320 | tf_op jit(solution)/shard_map/all_gather | solution.py:113
  413.7 8.1 copy-start.5
  766.7 9.3 %collective-permute-start = (bf16[512,256]{1,0:T(8,128)(2,1)S(1)}, bf16[512,256]{1,0:T(8,128)(2,1)S(1)}, u32[]{:S(2)}, u32[]{:S(2)}) collective-permute-start(bf16[512,256]{1,0:T(8,128)(2,1)S(1)} %get-tuple-element.481), channel_id=1, source_target_pairs={{0,1},{1,2},{2,3},{4,5},{5,6},{6,7},{8,9},{9,10},{10,11},{12,13},{... | collective-permute-start | bytes 786440 | tf_op jit(solution)/shard_map/while/body/eval_jaxpr/ppermute | solution.py:16
  777.6 2.1 copy-start.7
  782.9 1.4 copy-start.8
  784.2 9.5 %collective-permute-start = (bf16[512,256]{1,0:T(8,128)(2,1)S(1)}, bf16[512,256]{1,0:T(8,128)(2,1)S(1)}, u32[]{:S(2)}, u32[]{:S(2)}) collective-permute-start(bf16[512,256]{1,0:T(8,128)(2,1)S(1)} %get-tuple-element.481), channel_id=1, source_target_pairs={{0,1},{1,2},{2,3},{4,5},{5,6},{6,7},{8,9},{9,10},{10,11},{12,13},{... | collective-permute-start | bytes 786440 | tf_op jit(solution)/shard_map/while/body/eval_jaxpr/ppermute | solution.py:16
  795.2 2.1 copy-start.7
  800.5 1.4 copy-start.8
  801.8 8.6 %collective-permute-start = (bf16[512,256]{1,0:T(8,128)(2,1)S(1)}, bf16[512,256]{1,0:T(8,128)(2,1)S(1)}, u32[]{:S(2)}, u32[]{:S(2)}) collective-permute-start(bf16[512,256]{1,0:T(8,128)(2,1)S(1)} %get-tuple-element.481), channel_id=1, source_target_pairs={{0,1},{1,2},{2,3},{4,5},{5,6},{6,7},{8,9},{9,10},{10,11},{12,13},{... | collective-permute-start | bytes 786440 | tf_op jit(solution)/shard_map/while/body/eval_jaxpr/ppermute | solution.py:16
  812.0 2.1 copy-start.7
  817.2 1.4 copy-start.8
  818.6 2.9 copy-start.1
Sparse Core Ops, SparseCore 0:
  95.5 30.8 all-gather.14
  127.9 217.6 all-gather.8
  357.5 56.0 reduce-scatter.1
  415.7 63.4 all-gather.16
  480.5 216.8 all-gather.12
  698.8 44.5 all-gather.10
where the time goes:
time: 832 us; the launch traced here: 828 us
  waiting for transfers between devices  610 us (73%)
  local copies, waits for them, and re-layouts  74.6 us (9%)
  matrix products  71.7 us (9%)
  other arithmetic  24.5 us (3%)
  blocking collectives  20.1 us (2%)
  between operations  15 us (2%)
  starting transfers between devices  12.4 us (1%)
    all_gather x1, waiting for transfers between devices, shards(): lax.all_gather(query_weight, 'seq', axis=0, tiled=True)  218 us
    all_gather x1, waiting for transfers between devices, shards(): lax.all_gather(out_weight, 'seq', axis=1, tiled=True)  212 us
    all_gather x1, waiting for transfers between devices, shards(): lax.all_gather(kv_mine, 'seq', axis=0, tiled=True)  54.7 us
    reduce_scatter x1, waiting for transfers between devices, shards(): lax.psum_scatter(branch.astype(jnp.bfloat16), 'heads', scatter_dimension=...  54.5 us
    dynamic_update_slice x4, local copies, waits for them, and re-layouts, shards(): local_state, local_out = lax.scan(lightning_block, start_state, inputs)  50.5 us
    all_gather x1, waiting for transfers between devices, shards(): lax.all_gather(normed, 'heads', axis=1, tiled=True)  46 us
  transfers between devices with their start and end apart: 9, of which 9 were waited for; matrix products, arithmetic and copies ran while one was open for 2% of the time, Pallas kernels for 0%

commit v1 on v0

--- a/solution.py
+++ b/solution.py
@@ -8,6 +8,34 @@
 KVH = 4
 DH = 128
 BLOCK = 256
+
+
+def pass_node_all(x0):
+    item_now = lax.axis_size("heads")
+    local_now, spare, o_now = (item_now, lax.axis_index("heads"), x0.shape[1])
+    later = lax.dynamic_update_slice_in_dim(
+        jnp.zeros(
+            [src_i * local_now if nth == 1 else src_i for nth, src_i in enumerate(x0.shape)],
+            x0.dtype,
+        ),
+        x0,
+        spare * o_now,
+        axis=1,
+    )
+    r2 = y_new = x0
+    for num in range(1, local_now // 2 + 1):
+        r2 = lax.ppermute(r2, "heads", [(nth, (nth + 1) % local_now) for nth in range(local_now)])
+        later = lax.dynamic_update_slice_in_dim(
+            later, r2, (spare - num) % local_now * o_now, axis=1
+        )
+        if 2 * num < local_now:
+            y_new = lax.ppermute(
+                y_new, "heads", [(nth, (nth - 1) % local_now) for nth in range(local_now)]
+            )
+            later = lax.dynamic_update_slice_in_dim(
+                later, y_new, (spare + num) % local_now * o_now, axis=1
+            )
+    return later
 
 
 def from_behind(value, axis, steps):
@@ -109,11 +137,7 @@
         * lax.rsqrt(total_sq / D + 1e-05)[:, None]
         * norm_gain.astype(jnp.float32)[None, :]
     ).astype(jnp.bfloat16)
-    projected = jnp.dot(
-        lax.all_gather(normed, "heads", axis=1, tiled=True),
-        projection,
-        preferred_element_type=jnp.float32,
-    )
+    projected = jnp.dot(pass_node_all(normed), projection, preferred_element_type=jnp.float32)
     projected = projected.astype(jnp.bfloat16)
     queries = projected[:, :head_width].reshape(tok_rows, heads_here, DH)
     keys_values = projected[:, head_width:]

time: 832 us -> 784 us (0.942)
  waiting for transfers between devices: 610 us -> 553 us
  local copies, waits for them, and re-layouts: 74.6 us -> 83.2 us
    all_gather x1, waiting for transfers between devices: 54.7 us -> 0.01 us  [shards(): lax.all_gather(kv_mine, 'seq', axis=0, tiled=True)]
    ppermute x0 -> x3, waiting for transfers between devices: none -> 49.4 us  [the longest x2 49.4 us: pass_node_all(): lax.ppermute(r2, 'heads', [(nth, (nth + 1) % local_now) for nth in range(...]
    all_gather x1 -> x0, waiting for transfers between devices: 46 us -> none  [shards(): lax.all_gather(normed, 'heads', axis=1, tiled=True)]
  transfers between devices with their start and end apart: 9 -> 11, of which waited for: 9 -> 9; matrix products, arithmetic and copies ran while one was open for 2% -> 4% of each run, Pallas kernels for 0% -> 0%
where the time goes in v1:
time: 784 us; the launch traced here: 780 us
  waiting for transfers between devices  553 us (71%)
  local copies, waits for them, and re-layouts  83.2 us (11%)
  matrix products  71.6 us (9%)
  other arithmetic  25.7 us (3%)
  blocking collectives  19.9 us (3%)
  between operations  14.6 us (2%)
  starting transfers between devices  12 us (2%)
    all_gather x1, waiting for transfers between devices, shards(): lax.all_gather(query_weight, 'seq', axis=0, tiled=True)  212 us
    all_gather x1, waiting for transfers between devices, shards(): lax.all_gather(out_weight, 'seq', axis=1, tiled=True)  212 us
    reduce_scatter x1, waiting for transfers between devices, shards(): lax.psum_scatter(branch.astype(jnp.bfloat16), 'heads', scatter_dimension=...  54.6 us
    dynamic_update_slice x4, local copies, waits for them, and re-layouts, shards(): local_state, local_out = lax.scan(lightning_block, start_state, inputs)  50.5 us
    ppermute x2, waiting for transfers between devices, pass_node_all(): lax.ppermute(r2, 'heads', [(nth, (nth + 1) % local_now) for nth in range(...  49.4 us
  transfers between devices with their start and end apart: 11, of which 9 were waited for; matrix products, arithmetic and copies ran while one was open for 4% of the time, Pallas kernels for 0%

profile of v1, /device:TPU:0, one launch (start us, length us, event | category | flops | bytes accessed | tf_op | source)
XLA Modules:
  0.0 780.2 jit_solution(14996494444628762085)
XLA Ops:
  7.3 2.6 copy.92
  9.9 2.5 copy.93
  13.6 79.9 %while.34 = (s32[]{:T(128)}, f32[8,128,128]{2,1,0:T(8,128)}, f32[2,256,8,128]{1,0,3,2:T(2,128)}, f32[2,256,8]{1,2,0:T(8,128)S(1)}, bf16[2,256,8,128]{3,2,1,0:T(8...) while((s32[]{:T(128)}, f32[8,128,128]{2,1,0:T(8,128)}, ...), condition=%wide.region_3.4_spmd.clone, body=%wide.region_0.3_spmd.clone.sunk | while | flops 1078530048 | bytes 19645352 | solution.py:87
  14.5 2.3 constant_dynamic-slice_fusion.7
  16.8 3.5 convolution_bitcast_fusion.2
  21.6 2.2 convolution_add_fusion.2
  23.9 3.8 fusion.84
  27.7 3.3 copy.136
  31.0 22.0 %dynamic_update_slice.26 = f32[2,256,8,128]{1,0,3,2:T(2,128)} dynamic-update-slice(f32[2,256,8,128]{1,0,3,2:T(2,128)} %get-tuple-element.454, f32[1,256,8,128]{1,0,3,2:T(1,128)} %copy.136, s32[]{:T(128)S(6)} %copy.141, s32[]{:T(128)} %constant.133.clone.1..sunk, s32[]{:T(128)} %constant.133.clone.1..sunk, s32[]{:T(128)} %constant.133.clone.1..sunk) | dynamic-update-slice | bytes 2097156 | tf_op jit(solution)/shard_map/while/body/jit(dynamic_update_index_in_dim)/dynamic_update_slice | solution.py:87
  53.8 2.3 constant_dynamic-slice_fusion.7
  56.0 3.7 convolution_bitcast_fusion.2
  61.1 3.4 convolution_add_fusion.2
  64.5 3.8 fusion.84
  68.3 3.3 copy.136
  71.6 22.0 %dynamic_update_slice.26 = f32[2,256,8,128]{1,0,3,2:T(2,128)} dynamic-update-slice(f32[2,256,8,128]{1,0,3,2:T(2,128)} %get-tuple-element.454, f32[1,256,8,128]{1,0,3,2:T(1,128)} %copy.136, s32[]{:T(128)S(6)} %copy.141, s32[]{:T(128)} %constant.133.clone.1..sunk, s32[]{:T(128)} %constant.133.clone.1..sunk, s32[]{:T(128)} %constant.133.clone.1..sunk) | dynamic-update-slice | bytes 2097156 | tf_op jit(solution)/shard_map/while/body/jit(dynamic_update_index_in_dim)/dynamic_update_slice | solution.py:87
  93.5 1.8 convert_element_type.87
  96.3 3.9 reshape.219
  101.7 14.2 %all-reduce = bf16[32]{0:T(256)(128)(2,1)S(1)} all-reduce(bf16[32]{0:T(256)(128)(2,1)S(1)} %dynamic-update-slice), channel_id=2, replica_groups=mesh['groups'=2,'heads'=4,'seq'=4] {'seq'}, use_global_device_ids=true, to_apply=%add | all-reduce | flops 32 | bytes 128
  117.6 8.8 %all-gather.12.cloned.1.call-done = bf16[32,128,128]{2,1,0:T(8,128)(2,1)} async-done(((bf16[8,128,128]{2,1,0:T(8,128)(2,1)}), bf16[32,128,128]{2,1,0:T(8,128)(2,1)}) %all-gather.12.cloned.1.call-update) | async-done | bytes 1048592 | tf_op jit(solution)/shard_map/all_gather | solution.py:94
  127.9 4.7 multiply_reduce_fusion.2
  133.9 211.7 %all-gather.8.cloned.1.call-done = bf16[1024,6144]{1,0:T(8,128)(2,1)} async-done(((bf16[1024,1536]{1,0:T(8,128)(2,1)}), bf16[1024,6144]{1,0:T(8,128)(2,1)}) %all-gather.8.cloned.1.call-update) | async-done | bytes 12582928 | tf_op jit(solution)/shard_map/all_gather | solution.py:119
  345.6 11.7 %convolution_convert_fusion = bf16[512,6144]{1,0:T(8,128)(2,1)} fusion(bf16[512,1024]{0,1:T(8,128)(2,1)} %bitcast.181, bf16[1024,6144]{1,0:T(8,128)(2,1)} %all-gather.8.cloned.1.call-done), kind=kOutput, calls=%fused_computation.60 | convolution fusion | flops 6445596672 | bytes 19922944 | tf_op jit(solution)/shard_map/dot_general | solution.py:117
  359.0 54.6 %reduce-scatter.2.cloned.1.call-done = bf16[512,1536]{1,0:T(8,128)(2,1)} async-done(((bf16[512,6144]{1,0:T(8,128)(2,1)}), bf16[512,1536]{1,0:T(8,128)(2,1)}) %reduce-scatter.2.cloned.1.call-update) | async-done | bytes 1572880 | tf_op jit(solution)/shard_map/reduce_scatter | solution.py:129
  413.6 3.1 multiply_reduce_fusion
  416.7 5.7 psum.7
  422.5 3.4 broadcast_in_dim.151
  425.8 2.4 constant_dynamic-update-slice_fusion.3
  428.2 1.7 collective-permute-start.2
  429.9 33.7 %collective-permute-done.1 = bf16[512,1536]{1,0:T(8,128)(2,1)S(1)} collective-permute-done((bf16[512,1536]{1,0:T(8,128)(2,1)}, bf16[512,1536]{1,0:T(8,128)(2,1)S(1)}, u32[]{:S(2)}, u32[]{:S(2)}) %collective-permute-start.1) | collective-permute-done | bytes 1572896 | tf_op jit(solution)/shard_map/ppermute | solution.py:27
  465.2 2.7 constant_dynamic-update-slice_fusion.1
  467.9 15.6 %collective-permute-done.3 = bf16[512,1536]{1,0:T(8,128)(2,1)S(1)} collective-permute-done((bf16[512,1536]{1,0:T(8,128)(2,1)S(1)}, bf16[512,1536]{1,0:T(8,128)(2,1)S(1)}, u32[]{:S(2)}, u32[]{:S(2)}) %collective-permute-start.3) | collective-permute-done | bytes 1572896 | tf_op jit(solution)/shard_map/ppermute | solution.py:27
  484.9 212.5 %all-gather.10.cloned.1.call-done = bf16[6144,1024]{1,0:T(8,128)(2,1)} async-done(((bf16[1536,1024]{1,0:T(8,128)(2,1)}), bf16[6144,1024]{1,0:T(8,128)(2,1)}) %all-gather.10.cloned.1.call-update) | async-done | bytes 12582928 | tf_op jit(solution)/shard_map/all_gather | solution.py:125
  697.4 15.6 %fusion.43 = bf16[512,1280]{1,0:T(8,128)(2,1)S(1)} fusion(bf16[512,6144]{1,0:T(8,128)(2,1)} %constant_dynamic-update-slice_fusion, bf16[6144,256]{1,0:T(8,128)(2,1)} %bitcast.188, bf16[6144,1024]{1,0:T(8,128)(2,1)} %all-gather.10.cloned.1.call-done), kind=kOutput, calls=%fused_computation.71 | convolution fusion | flops 8085176320 | bytes 23330816 | tf_op jit(solution)/shard_map/dot_general | solution.py:140
  714.7 2.3 fusion.39
  717.0 3.9 fusion.49
  720.9 49.9 %while.33 = (s32[]{:T(128)}, bf16[512,256]{1,0:T(8,128)(2,1)S(1)}, f32[8,512]{1,0:T(8,128)S(1)}, f32[8,512]{1,0:T(8,128)S(1)}, f32[8,512,128]{2,1,0:T(8,128)}, /...) while((s32[]{:T(128)}, bf16[512,256]{1,0:T(8,128)(2,1)S(1)}, ...), condition=%wide.region_18.19_spmd.clone, body=%wide.region_15.18_spmd.clone.sunk | while | flops 1102587904 | bytes 50341096 | solution.py:184
  722.5 5.7 collective-permute-done
  729.8 2.0 fusion.79
  731.9 3.1 multiply_add_fusion.5
  736.4 4.4 collective-permute-start
  741.0 4.8 collective-permute-done
  747.4 2.0 fusion.79
  749.5 3.1 multiply_add_fusion.5
  754.0 4.4 collective-permute-start
  758.7 4.0 collective-permute-done
  764.2 2.0 fusion.79
  766.3 3.1 multiply_add_fusion.5
  770.8 2.9 copy_bitcast_fusion.11
  (132 shorter events, 29.2 us)
Async XLA Ops:
  7.2 350.3 %copy-start = (bf16[4,1536,256]{2,1,0:T(8,128)(2,1)S(1)}, bf16[4,1536,256]{2,1,0:T(8,128)(2,1)}, u32[]{:S(2)}) copy-start(bf16[4,1536,256]{2,1,0:T(8,128)(2,1)} %param.21) | copy-start | bytes 9437188
  7.2 119.2 %all-gather.12.cloned.1.call-start = ((), (), s32[]{:S(2)}) async-start(), calls=%async_computation.4 | async-start | bytes 1310720 | tf_op jit(solution)/shard_map/all_gather | solution.py:94
  7.2 5.1 copy-start.6
  7.3 6.4 copy-start.9
  16.7 4.9 copy-start.2
  21.6 2.2 copy-start.3
  56.0 5.0 copy-start.2
  61.0 3.4 copy-start.3
  95.3 4.9 copy-start.11
  95.4 250.2 %all-gather.8.cloned.1.call-start = ((), (), s32[]{:S(2)}) async-start(), calls=%async_computation.1 | async-start | bytes 15728640 | tf_op jit(solution)/shard_map/all_gather | solution.py:119
  96.1 317.5 %reduce-scatter.2.cloned.1.call-start = ((), (), s32[]{:S(2)}) async-start(), calls=%async_computation.2 | async-start | bytes 7864320 | tf_op jit(solution)/shard_map/reduce_scatter | solution.py:129
  357.4 1.6 copy-start.10
  357.4 127.5 %all-gather.14.cloned.1.call-start = ((), (), s32[]{:S(2)}) async-start(), calls=%async_computation.5 | async-start | bytes 3932160 | tf_op jit(solution)/shard_map/all_gather | solution.py:126
  358.4 55.2 %copy-start.4 = (bf16[512,1536]{1,0:T(8,128)(2,1)S(1)}, bf16[512,1536]{1,0:T(8,128)(2,1)}, u32[]{:S(2)}) copy-start(bf16[512,1536]{1,0:T(8,128)(2,1)} %param.17) | copy-start | bytes 4718596
  358.4 338.9 %all-gather.10.cloned.1.call-start = ((), (), s32[]{:S(2)}) async-start(), calls=%async_computation.3 | async-start | bytes 15728640 | tf_op jit(solution)/shard_map/all_gather | solution.py:125
  422.5 3.4 copy-start.5
  428.2 35.5 %collective-permute-start.1 = (bf16[512,1536]{1,0:T(8,128)(2,1)}, bf16[512,1536]{1,0:T(8,128)(2,1)S(1)}, u32[]{:S(2)}, u32[]{:S(2)}) collective-permute-start(bf16[512,1536]{1,0:T(8,128)(2,1)} %get-tuple-element.315), channel_id=1, source_target_pairs={{0,4},{4,8},{8,12},{12,0},{1,5},{5,9},{9,13},{13,1},{2,6},{6,10},{... | collective-permute-start | bytes 4718600 | tf_op jit(solution)/shard_map/ppermute | solution.py:27
  428.2 37.0 %collective-permute-start.2 = (bf16[512,1536]{1,0:T(8,128)(2,1)}, bf16[512,1536]{1,0:T(8,128)(2,1)}, u32[]{:S(2)}, u32[]{:S(2)}) collective-permute-start(bf16[512,1536]{1,0:T(8,128)(2,1)} %get-tuple-element.315), channel_id=1, source_target_pairs={{0,12},{4,0},{8,4},{12,8},{1,13},{5,1},{9,5},{13,9},{2,14},{6,2},{... | collective-permute-start | bytes 4718600 | tf_op jit(solution)/shard_map/ppermute | solution.py:32
  463.7 19.8 %collective-permute-start.3 = (bf16[512,1536]{1,0:T(8,128)(2,1)S(1)}, bf16[512,1536]{1,0:T(8,128)(2,1)S(1)}, u32[]{:S(2)}, u32[]{:S(2)}) collective-permute-start(bf16[512,1536]{1,0:T(8,128)(2,1)S(1)} %collective-permute-done.1), channel_id=1, source_target_pairs={{0,4},{4,8},{8,12},{12,0},{1,5},{5,9},{9,13},{13,1},{2,6},{6,10},{... | collective-permute-start | bytes 4718600 | tf_op jit(solution)/shard_map/ppermute | solution.py:27
  721.0 7.3 collective-permute-start
  729.8 2.1 copy-start.7
  735.0 1.4 copy-start.8
  736.4 9.5 %collective-permute-start = (bf16[512,256]{1,0:T(8,128)(2,1)S(1)}, bf16[512,256]{1,0:T(8,128)(2,1)S(1)}, u32[]{:S(2)}, u32[]{:S(2)}) collective-permute-start(bf16[512,256]{1,0:T(8,128)(2,1)S(1)} %get-tuple-element.483), channel_id=1, source_target_pairs={{0,1},{1,2},{2,3},{4,5},{5,6},{6,7},{8,9},{9,10},{10,11},{12,13},{... | collective-permute-start | bytes 786440 | tf_op jit(solution)/shard_map/while/body/eval_jaxpr/ppermute | solution.py:44
  747.4 2.1 copy-start.7
  752.7 1.4 copy-start.8
  754.0 8.7 %collective-permute-start = (bf16[512,256]{1,0:T(8,128)(2,1)S(1)}, bf16[512,256]{1,0:T(8,128)(2,1)S(1)}, u32[]{:S(2)}, u32[]{:S(2)}) collective-permute-start(bf16[512,256]{1,0:T(8,128)(2,1)S(1)} %get-tuple-element.483), channel_id=1, source_target_pairs={{0,1},{1,2},{2,3},{4,5},{5,6},{6,7},{8,9},{9,10},{10,11},{12,13},{... | collective-permute-start | bytes 786440 | tf_op jit(solution)/shard_map/while/body/eval_jaxpr/ppermute | solution.py:44
  764.2 2.1 copy-start.7
  769.5 1.4 copy-start.8
  770.8 2.9 copy-start.1
Sparse Core Ops, SparseCore 0:
  95.5 30.8 all-gather.11
  127.9 217.6 all-gather.7
  357.5 56.0 reduce-scatter.1
  415.6 63.4 all-gather.13
  480.5 216.8 all-gather.9
